TPU v7x, 256 devices: a whole 4x4x8 slice. The times are simulated.
256 devices in a mesh: section: 2 (over core), seq: 16 (over x, y), exp: 8 (over z).
Axes of the slice: x: 4, y: 4, z: 8, core: 2. Of those that a mesh axis runs over, the one named last changes fastest.
Arguments:
- hidden_in: bfloat16 [2048, 2048], P('seq'), may hold values from -6 to 6
- seg_ids: int32 [2048], P('seq'), may hold values from 0 to 7, never falling along the last dimension, each value on 1 to 1024 neighbouring positions
- attn_gain: float32 [2048], replicated, may hold values from 0.25 to 1.75
- w_query: bfloat16 [2048, 2048], P(None, ('section', 'exp'))
- w_key: bfloat16 [2048, 2048], P(None, ('section', 'exp'))
- w_value: bfloat16 [2048, 2048], P(None, ('section', 'exp')), may hold values from -0.125 to 0.125
- w_out: bfloat16 [2048, 2048], P(('section', 'exp')), may hold values from -0.5 to 0.5
- moe_gain: float32 [2048], replicated, may hold values from 0.25 to 1.75
- expert_ids: int32 [2048, 8], P(('seq', 'exp')), may hold values from 0 to 63, all different within a row; in each aligned block of 16 rows (0 to 15, 16 to 31, ...) at most 4 rows name the same one
- route_weights: float32 [2048, 8], P(('seq', 'exp')), may hold values from 0.1 to 0.6
- gate_halves: bfloat16 [128, 2048, 512], P(('seq', 'exp'), None, 'section'), may hold values from -0.125 to 0.125
- up_halves: bfloat16 [128, 2048, 512], P(('seq', 'exp'), None, 'section'), may hold values from -0.125 to 0.125
- down_halves: bfloat16 [128, 512, 2048], P(('seq', 'exp'), 'section'), may hold values from -0.1875 to 0.1875
Outputs:
- layer_out: bfloat16 [2048, 2048], P(('seq', 'exp'))
Inputs may be any that keep to these rules, and one draw needn't show every extreme that they name: `seg_ids`: prompt numbers never fall along the batch; each prompt holds 1 to 1024 tokens, and one holds exactly 1024. `expert_ids`: A token's 8 experts are distinct. In each aligned block of 16 tokens (the tokens of one device along seq and exp), no expert is chosen by more than 4 of the block's tokens, a bound that some block reaches.
All inputs are finite; a program needn't handle non-finite values.
Results may differ from a plain program's by a relative error of at most 0.012.
Values may be sent and summed in bfloat16 or wider, within the bound.
No kernel may reach another device: no remote copies, remote signals or barrier semaphores. Data moves between devices by JAX's collectives and lax.ppermute only.
A program may use at most 64 MiB of HBM per device.

v0:
```python
import math
import jax
import jax.numpy as jnp
from jax import lax
from jax.sharding import PartitionSpec as P

epsilon = 1e-05
rope_base = 10000.0


def rms_scale(rows, gain):
    wide = rows.astype(jnp.float32)
    inverse = lax.rsqrt(jnp.mean(wide * wide, axis=-1, keepdims=True) + epsilon)
    return (wide * inverse * gain).astype(jnp.bfloat16)


def rotate(values, positions):
    half_dim = values.shape[-1] // 2
    frequency = rope_base ** (-2.0 * jnp.arange(half_dim, dtype=jnp.float32) / values.shape[-1])
    angles = positions.astype(jnp.float32)[:, None] * frequency[None, :]
    cosine = jnp.cos(angles)
    sine_part = jnp.sin(angles)
    first_half = values[:, :half_dim]
    second_half = values[:, half_dim:]
    return jnp.concatenate(
        [
            first_half * cosine - second_half * sine_part,
            second_half * cosine + first_half * sine_part,
        ],
        axis=-1,
    )


def per_device(
    hidden_in,
    seg_ids,
    attn_gain,
    w_query,
    w_key,
    w_value,
    w_out,
    moe_gain,
    expert_ids,
    route_weights,
    gate_halves,
    up_halves,
    down_halves,
):
    tok_seq = hidden_in.shape[0]
    width = hidden_in.shape[1]
    head_dim = w_query.shape[1]
    positions = lax.axis_index("seq") * tok_seq + jnp.arange(tok_seq, dtype=jnp.int32)
    normed = rms_scale(hidden_in, attn_gain)
    query_rows = rotate(
        jnp.dot(normed, w_query, preferred_element_type=jnp.float32), positions
    ).astype(jnp.bfloat16)
    key_rows = rotate(jnp.dot(normed, w_key, preferred_element_type=jnp.float32), positions).astype(
        jnp.bfloat16
    )
    value_rows = jnp.dot(normed, w_value, preferred_element_type=jnp.float32).astype(jnp.bfloat16)
    score_scale = 1.0 / math.sqrt(head_dim)
    run_max = jnp.full((tok_seq,), -1e30, jnp.float32)
    piece_keys = lax.all_gather(key_rows, "seq", axis=0, tiled=True)
    piece_values = lax.all_gather(value_rows, "seq", axis=0, tiled=True)
    key_segs = lax.all_gather(seg_ids, "seq", axis=0, tiled=True)
    piece_rows = piece_keys.shape[0]
    scores = (
        lax.dot_general(
            query_rows, piece_keys, (((1,), (1,)), ((), ())), preferred_element_type=jnp.float32
        )
        * score_scale
    )
    key_pos = jnp.arange(piece_rows, dtype=jnp.int32)
    allowed = (seg_ids[:, None] == key_segs[None, :]) & (key_pos[None, :] <= positions[:, None])
    masked = jnp.where(allowed, scores, -1e30)
    new_max = jnp.maximum(run_max, jnp.max(masked, axis=1))
    weights = jnp.where(allowed, jnp.exp(masked - new_max[:, None]), 0.0)
    run_total = jnp.sum(weights, axis=1)
    weighted_sum = jnp.dot(
        weights.astype(jnp.bfloat16), piece_values, preferred_element_type=jnp.float32
    )
    run_max, run_total, weighted_sum = (new_max, run_total, weighted_sum)
    head_out = (weighted_sum / run_total[:, None]).astype(jnp.bfloat16)
    partial_value = jnp.dot(head_out, w_out, preferred_element_type=jnp.float32)
    tok_dev = tok_seq // lax.axis_size("exp")
    own_start = lax.axis_index("exp") * tok_dev
    summed = lax.psum(partial_value, ("section", "exp"))
    summed = lax.dynamic_slice_in_dim(summed, own_start, tok_dev, 0)
    own_rows = lax.dynamic_slice_in_dim(hidden_in, own_start, tok_dev, 0)
    residual = (own_rows.astype(jnp.float32) + summed).astype(jnp.bfloat16)
    moe_in = rms_scale(residual, moe_gain)
    experts = lax.axis_size("seq") * lax.axis_size("exp") // 2
    top_count = expert_ids.shape[1]
    capacity = min(tok_dev, max(2, 2 * tok_dev * top_count // experts))
    row_count = tok_dev * top_count
    flat_ids = expert_ids.reshape(row_count)
    one_hot = (flat_ids[:, None] == jnp.arange(experts, dtype=jnp.int32)[None, :]).astype(jnp.int32)
    slot_rank = jnp.sum((jnp.cumsum(one_hot, axis=0) - one_hot) * one_hot, axis=1)
    slot_index = flat_ids * capacity + slot_rank
    placed = slot_index[:, None] == jnp.arange(experts * capacity, dtype=jnp.int32)[None, :]
    repeated = jnp.repeat(moe_in, top_count, axis=0)
    outgoing = lax.dot_general(
        placed.astype(jnp.bfloat16),
        repeated,
        (((0,), (0,)), ((), ())),
        preferred_element_type=jnp.float32,
    ).astype(jnp.bfloat16)
    row_token = jnp.arange(row_count, dtype=jnp.int32) // top_count
    token_hot = (row_token[None, :] == jnp.arange(tok_dev, dtype=jnp.int32)[:, None]).astype(
        jnp.float32
    )
    weighted = token_hot * route_weights.reshape(row_count)[None, :]
    combine = jnp.dot(weighted, placed.astype(jnp.float32), precision=lax.Precision.HIGHEST)
    doubled = jnp.broadcast_to(
        outgoing.reshape(experts, 1, capacity, width), (experts, 2, capacity, width)
    ).reshape(2 * experts, capacity, width)
    arrived = lax.all_to_all(doubled, ("seq", "exp"), split_axis=0, concat_axis=0, tiled=True)
    flat_rows = arrived.reshape(-1, width)
    gate_proj = jnp.dot(flat_rows, gate_halves[0], preferred_element_type=jnp.float32)
    up_proj = jnp.dot(flat_rows, up_halves[0], preferred_element_type=jnp.float32)
    activated = (jax.nn.silu(gate_proj) * up_proj).astype(jnp.bfloat16)
    returned = lax.all_to_all(
        jnp.dot(activated, down_halves[0], preferred_element_type=jnp.float32)
        .astype(jnp.bfloat16)
        .reshape(arrived.shape),
        ("seq", "exp"),
        split_axis=0,
        concat_axis=0,
        tiled=True,
    )
    halves_sum = jnp.sum(
        returned.reshape(experts, 2, capacity, width).astype(jnp.float32), axis=1
    ).reshape(experts * capacity, width)
    moe_part = jnp.dot(combine, halves_sum, precision=lax.Precision.HIGHEST)
    moe_total = lax.psum(moe_part, "section")
    return (residual.astype(jnp.float32) + moe_total).astype(jnp.bfloat16)


def solution(mesh):
    in_specs = (
        P("seq", None),
        P("seq"),
        P(),
        P(None, ("section", "exp")),
        P(None, ("section", "exp")),
        P(None, ("section", "exp")),
        P(("section", "exp"), None),
        P(),
        P(("seq", "exp"), None),
        P(("seq", "exp"), None),
        P(("seq", "exp"), None, "section"),
        P(("seq", "exp"), None, "section"),
        P(("seq", "exp"), "section", None),
    )
    out_specs = P(("seq", "exp"), None)
    return jax.shard_map(
        per_device, mesh=mesh, in_specs=in_specs, out_specs=out_specs, check_vma=False
    )
```

profile of v0, /device:TPU:1, one launch (start us, length us, event | category | flops | bytes accessed | tf_op | source)
XLA Modules:
  0.0 376.0 jit_solution(10940934380651629049)
XLA Ops:
  6.5 0.0 copy-start
  6.5 0.0 all-reduce.3.cloned.1.call-start
  6.6 1.3 fusion.4
  7.9 1.6 fusion.74
  9.5 0.0 copy-start.2
  9.5 0.0 copy-start.7
  9.6 0.0 copy-start.8
  9.6 1.7 fusion.76
  11.3 0.2 fusion.52
  11.5 20.5 %all_gather.10 = bf16[2048,128]{0,1:T(8,128)(2,1)S(1)} all-gather(bf16[128,128]{0,1:T(8,128)(2,1)S(1)} %pad_maximum_fusion), channel_id=1, replica_groups=mesh['section'=2,'seq'=16,'exp'=8] {'seq'}, dimensions={0}, use_global_device_ids=true | all-gather | bytes 557056 | tf_op jit(solution)/shard_map/all_gather | solution.py:63
  32.0 15.7 %all-gather = s32[16,1,128]{2,1,0:T(1,128)S(1)} all-gather(s32[1,1,128]{2,1,0:T(1,128)S(1)} %bitcast.33), channel_id=1, replica_groups=mesh['section'=2,'seq'=16,'exp'=8] {'seq'}, dimensions={0}, use_global_device_ids=true | all-gather | bytes 8704 | tf_op jit(solution)/shard_map/all_gather | solution.py:65
  47.8 0.5 fusion.78
  48.3 0.4 convolution_convert_fusion.2
  48.7 16.1 %all_gather.11 = bf16[2048,128]{1,0:T(8,128)(2,1)S(1)} all-gather(bf16[128,128]{1,0:T(8,128)(2,1)S(1)} %convolution_convert_fusion.2), channel_id=1, replica_groups=mesh['section'=2,'seq'=16,'exp'=8] {'seq'}, dimensions={0}, use_global_device_ids=true | all-gather | bytes 557056 | tf_op jit(solution)/shard_map/all_gather | solution.py:64
  64.8 0.4 fusion.13
  65.2 0.0 copy-start.3
  65.2 2.8 fusion.3
  68.0 0.0 all-reduce.3.cloned.1.call-update
  68.1 0.1 copy.19
  68.1 0.1 reshape.82
  68.2 0.1 fusion.42
  68.3 0.2 reduce_window_sum.11
  68.5 0.2 select_reduce_fusion
  68.7 128.0 %all-reduce.3.cloned.1.call-done = f32[128,2048]{1,0:T(8,128)} async-done(((f32[128,2048]{1,0:T(8,128)}), f32[128,2048]{1,0:T(8,128)}) %all-reduce.3.cloned.1.call-update) | async-done | bytes 1048592 | tf_op jit(solution)/shard_map/psum | solution.py:87
  196.7 1.0 fusion.35
  197.7 0.1 fusion.37
  197.8 0.5 convolution_convert_fusion.1
  198.4 0.4 broadcast_in_dim.19
  198.8 1.2 broadcast_in_dim.20
  200.1 63.0 %all_to_all.10 = bf16[128,4,2048]{2,1,0:T(4,128)(2,1)S(1)} all-to-all(bf16[128,4,2048]{2,1,0:T(4,128)(2,1)S(1)} %bitcast.29), channel_id=1, replica_groups=mesh['section'=2,'seq'=16,'exp'=8] {'seq','exp'}, dimensions={0} | all-to-all | bytes 4194304 | tf_op jit(solution)/shard_map/all_to_all | solution.py:117
  263.1 2.1 reshape.85
  265.1 3.5 fusion.10
  268.7 0.0 copy-done
  268.7 5.0 %convolution_convert_fusion = bf16[512,2048]{1,0:T(8,128)(2,1)} fusion(bf16[512,2048]{1,0:T(8,128)(2,1)S(1)} %copy-done.1, bf16[1,256,2048]{2,1,0:T(8,128)(2,1)S(1)} %copy-done, bf16[1,2048,256]{2,1,0:T(8,128)(2,1)} %param.24, f32[512,256]{1,0:T(8,128)} %fusion.10), kind=kOutput, calls=%fused_computation.1 | convolution fusion | flops 1075576832 | bytes 6815744 | tf_op jit(solution)/shard_map/dot_general | solution.py:123
  273.7 4.1 %reshape.86 = bf16[128,4,2048]{2,1,0:T(4,128)(2,1)} reshape(bf16[512,2048]{1,0:T(8,128)(2,1)} %convolution_convert_fusion) | data formatting | bytes 4194304 | tf_op jit(solution)/shard_map/reshape | solution.py:125
  277.8 6.7 %all-to-all-start.1 = ((bf16[128,4,2048]{2,1,0:T(4,128)(2,1)}), bf16[128,4,2048]{2,1,0:T(4,128)(2,1)S(1)}, u32[]{:S(2)}, u32[]{:S(2)}) async-start(bf16[128,4,2048]{2,1,0:T(4,128)(2,1)} %reshape.86), calls=%async_computation.1 | async-start | bytes 4194304 | tf_op jit(solution)/shard_map/all_to_all | solution.py:122
  284.6 0.2 all-reduce.5.cloned.1.call-start
  284.8 0.0 copy-done.6
  284.8 0.1 copy.18
  284.9 0.1 mul.147
  285.0 0.2 fusion.39
  285.2 49.4 %all-to-all-done.1 = bf16[128,4,2048]{2,1,0:T(4,128)(2,1)S(1)} async-done(((bf16[128,4,2048]{2,1,0:T(4,128)(2,1)}), bf16[128,4,2048]{2,1,0:T(4,128)(2,1)S(1)}, u32[]{:S(2)}, u32[]{:S(2)}) %all-to-all-start.1) | async-done | bytes 2097184 | tf_op jit(solution)/shard_map/all_to_all | solution.py:122
  334.5 2.7 convert_reduce_fusion
  337.2 2.0 reshape.87
  339.2 1.8 fusion.79
  341.0 0.0 all-reduce.5.cloned.1.call-update
  341.0 26.6 %all-reduce.5.cloned.1.call-done = f32[16,2048]{1,0:T(8,128)} async-done(((f32[16,2048]{1,0:T(8,128)}), f32[16,2048]{1,0:T(8,128)}) %all-reduce.5.cloned.1.call-update) | async-done | bytes 131088 | tf_op jit(solution)/shard_map/psum | solution.py:135
  367.6 1.5 fusion.38
  (20 shorter events, 0.1 us)
Async XLA Ops:
  6.5 262.1 %copy-start = (bf16[1,256,2048]{2,1,0:T(8,128)(2,1)S(1)}, bf16[1,256,2048]{2,1,0:T(8,128)(2,1)}, u32[]{:S(2)}) copy-start(bf16[1,256,2048]{2,1,0:T(8,128)(2,1)} %param.25) | copy-start | bytes 3145732
  6.5 25.5 %copy-start.4 = (s32[128]{0:T(128)S(1)}, s32[128]{0:T(128)}, u32[]{:S(2)}) copy-start(s32[128]{0:T(128)} %param.14) | copy-start | bytes 1540
  6.5 190.1 %all-reduce.3.cloned.1.call-start = ((), (), s32[]{:S(2)}) async-start(), calls=%async_computation.2 | async-start | bytes 2097152 | tf_op jit(solution)/shard_map/psum | solution.py:87
  9.5 38.8 %copy-start.2 = (bf16[128,2048]{1,0:T(8,128)(2,1)S(1)}, bf16[128,2048]{1,0:T(8,128)(2,1)}, u32[]{:S(2)}) copy-start(bf16[128,2048]{1,0:T(8,128)(2,1)} %param.13) | copy-start | bytes 1572868
  9.5 38.8 %copy-start.7 = (bf16[2048,128]{1,0:T(8,128)(2,1)S(1)}, bf16[2048,128]{1,0:T(8,128)(2,1)}, u32[]{:S(2)}) copy-start(bf16[2048,128]{1,0:T(8,128)(2,1)} %param.18) | copy-start | bytes 1572868
  9.6 38.8 %copy-start.8 = (f32[2048]{0:T(1024)S(1)}, f32[2048]{0:T(1024)}, u32[]{:S(2)}) copy-start(f32[2048]{0:T(1024)} %param.15) | copy-start | bytes 24580
  65.2 2.8 copy-start.5
  65.2 132.5 %copy-start.3 = (f32[2048]{0:T(1024)S(1)}, f32[2048]{0:T(1024)}, u32[]{:S(2)}) copy-start(f32[2048]{0:T(1024)} %param.20) | copy-start | bytes 24580
  265.1 3.5 copy-start.1
  277.8 7.0 %copy-start.6 = (f32[16,8]{0,1:T(8,128)S(1)}, f32[16,8]{0,1:T(8,128)}, u32[]{:S(2)}) copy-start(f32[16,8]{0,1:T(8,128)} %param.22) | copy-start | bytes 1540
  277.8 56.7 %all-to-all-start.1 = ((bf16[128,4,2048]{2,1,0:T(4,128)(2,1)}), bf16[128,4,2048]{2,1,0:T(4,128)(2,1)S(1)}, u32[]{:S(2)}, u32[]{:S(2)}) async-start(bf16[128,4,2048]{2,1,0:T(4,128)(2,1)} %reshape.86), calls=%async_computation.1 | async-start | bytes 4194304 | tf_op jit(solution)/shard_map/all_to_all | solution.py:122
  284.6 83.1 %all-reduce.5.cloned.1.call-start = ((), (), s32[]{:S(2)}) async-start(), calls=%async_computation.3 | async-start | bytes 262144 | tf_op jit(solution)/shard_map/psum | solution.py:135
Sparse Core Ops, SparseCore 0:
  68.2 128.4 all-reduce.2
  341.1 26.4 all-reduce.4
where the time goes:
time: 377 us; the launch traced here: 376 us
  waiting for transfers between devices  204 us (54%)
  blocking collectives  115 us (31%)
  matrix products  18 us (5%)
  between operations  13.6 us (4%)
  local copies, waits for them, and re-layouts  10.2 us (3%)
  other arithmetic  7.82 us (2%)
  starting transfers between devices  6.96 us (2%)
    psum x1, waiting for transfers between devices, per_device(): summed = lax.psum(partial_value, ('section', 'exp'))  128 us
    all_to_all x1, blocking collectives, per_device(): lax.all_to_all(doubled, ('seq', 'exp'), split_axis=0, concat_axis=0, tile...  63 us
    all_to_all x1, waiting for transfers between devices, per_device(): lax.all_to_all(jnp.dot(activated, down_halves[0], preferred_element_type=...  49.4 us
    psum x1, waiting for transfers between devices, per_device(): moe_total = lax.psum(moe_part, 'section')  26.6 us
    all_gather x1, blocking collectives, per_device(): piece_keys = lax.all_gather(key_rows, 'seq', axis=0, tiled=True)  20.5 us
    all_gather x1, blocking collectives, per_device(): piece_values = lax.all_gather(value_rows, 'seq', axis=0, tiled=True)  16.1 us
    all_gather x1, blocking collectives, per_device(): key_segs = lax.all_gather(seg_ids, 'seq', axis=0, tiled=True)  15.7 us
  transfers between devices with their start and end apart: 3, of which 3 were waited for; matrix products, arithmetic and copies ran while one was open for 0% of the time, Pallas kernels for 0%

commit v1 on v0

--- a/solution.py
+++ b/solution.py
@@ -6,6 +6,28 @@
 
 epsilon = 1e-05
 rope_base = 10000.0
+
+
+def joined_along(parts, dim):
+    lengths = list(parts.shape[1:])
+    lengths[dim] *= parts.shape[0]
+    return jnp.moveaxis(parts, 0, dim).reshape(lengths)
+
+
+def collect(value, axis, dim):
+    length = lax.axis_size(axis)
+    pairs = [(i, (i + 1) % length) for i in range(length)]
+    back = [(b, a) for a, b in pairs]
+    lower, upper = ([], [])
+    for lap in range(length - 1):
+        if lap % 2 == 0:
+            lower.append(lax.ppermute(lower[-1] if lower else value, axis, pairs))
+        else:
+            upper.append(lax.ppermute(upper[-1] if upper else value, axis, back))
+    blocks = jnp.stack([*lower[::-1], value, *upper])
+    shift = lax.axis_index(axis) - len(lower)
+    blocks = blocks[(jnp.arange(length) - shift) % length]
+    return joined_along(blocks, dim)
 
 
 def rms_scale(rows, gain):
@@ -61,7 +83,7 @@
     score_scale = 1.0 / math.sqrt(head_dim)
     run_max = jnp.full((tok_seq,), -1e30, jnp.float32)
     piece_keys = lax.all_gather(key_rows, "seq", axis=0, tiled=True)
-    piece_values = lax.all_gather(value_rows, "seq", axis=0, tiled=True)
+    piece_values = collect(value_rows, "seq", 0)
     key_segs = lax.all_gather(seg_ids, "seq", axis=0, tiled=True)
     piece_rows = piece_keys.shape[0]
     scores = (

time: 377 us -> 408 us (1.082)
  starting transfers between devices: 6.96 us -> 40.5 us
  blocking collectives: 115 us -> 98.5 us
  local copies, waits for them, and re-layouts: 10.2 us -> 21.7 us
    ppermute x0 -> x15, starting transfers between devices: none -> 33.4 us  [the longest x7 29.9 us: collect(): upper.append(lax.ppermute(upper[-1] if upper else value, axis, back))]
    all_gather x1 -> x0, blocking collectives: 16.1 us -> none  [per_device(): piece_values = lax.all_gather(value_rows, 'seq', axis=0, tiled=True)]
    unnamed x20 -> x35, local copies, waits for them, and re-layouts: 0.19 us -> 9.38 us
    ppermute x0 -> x15, waiting for transfers between devices: none -> 4.54 us  [the longest x7 4.51 us: collect(): upper.append(lax.ppermute(upper[-1] if upper else value, axis, back))]
  transfers between devices with their start and end apart: 3 -> 18, of which waited for: 3 -> 8; matrix products, arithmetic and copies ran while one was open for 0% -> 3% of each run, Pallas kernels for 0% -> 0%
where the time goes in v1:
time: 408 us; the launch traced here: 407 us
  waiting for transfers between devices  207 us (51%)
  blocking collectives  98.5 us (24%)
  starting transfers between devices  40.5 us (10%)
  local copies, waits for them, and re-layouts  21.7 us (5%)
  matrix products  17.9 us (4%)
  between operations  13.7 us (3%)
  other arithmetic  7.87 us (2%)
    psum x1, waiting for transfers between devices, per_device(): summed = lax.psum(partial_value, ('section', 'exp'))  126 us
    all_to_all x1, blocking collectives, per_device(): lax.all_to_all(doubled, ('seq', 'exp'), split_axis=0, concat_axis=0, tile...  63 us
    all_to_all x1, waiting for transfers between devices, per_device(): lax.all_to_all(jnp.dot(activated, down_halves[0], preferred_element_type=...  49.3 us
    ppermute x7, starting transfers between devices, collect(): upper.append(lax.ppermute(upper[-1] if upper else value, axis, back))  29.9 us
    psum x1, waiting for transfers between devices, per_device(): moe_total = lax.psum(moe_part, 'section')  26.6 us
    all_gather x1, blocking collectives, per_device(): piece_keys = lax.all_gather(key_rows, 'seq', axis=0, tiled=True)  19.6 us
    all_gather x1, blocking collectives, per_device(): key_segs = lax.all_gather(seg_ids, 'seq', axis=0, tiled=True)  15.9 us
    unnamed x35, local copies, waits for them, and re-layouts  9.38 us
  transfers between devices with their start and end apart: 18, of which 8 were waited for; matrix products, arithmetic and copies ran while one was open for 3% of the time, Pallas kernels for 0%

profile of v1, /device:TPU:1, one launch (start us, length us, event | category | flops | bytes accessed | tf_op | source)
XLA Modules:
  0.0 407.2 jit_solution(10836627285836656292)
XLA Ops:
  6.6 1.4 fusion.4
  8.0 1.6 convolution_convert_fusion.2
  9.6 2.2 collective-permute-start
  11.8 3.7 collective-permute-start.8
  15.5 1.6 fusion.76
  17.9 19.6 %all_gather.7 = bf16[2048,128]{0,1:T(8,128)(2,1)S(1)} all-gather(bf16[128,128]{0,1:T(8,128)(2,1)S(1)} %pad_maximum_fusion), channel_id=1, replica_groups=mesh['section'=2,'seq'=16,'exp'=8] {'seq'}, dimensions={0}, use_global_device_ids=true | all-gather | bytes 557056 | tf_op jit(solution)/shard_map/all_gather | solution.py:85
  37.5 1.2 collective-permute-start.2
  38.8 15.9 %all-gather = s32[16,1,128]{2,1,0:T(1,128)S(1)} all-gather(s32[1,1,128]{2,1,0:T(1,128)S(1)} %bitcast.69), channel_id=1, replica_groups=mesh['section'=2,'seq'=16,'exp'=8] {'seq'}, dimensions={0}, use_global_device_ids=true | all-gather | bytes 8704 | tf_op jit(solution)/shard_map/all_gather | solution.py:87
  54.7 1.5 collective-permute-start.9
  56.7 1.1 collective-permute-done.9
  57.8 4.5 %collective-permute-start.10 = (bf16[128,128]{1,0:T(8,128)(2,1)S(1)}, bf16[128,128]{1,0:T(8,128)(2,1)S(1)}, u32[]{:S(2)}, u32[]{:S(2)}) collective-permute-start(bf16[128,128]{1,0:T(8,128)(2,1)S(1)} %collective-permute-done.9), channel_id=1, source_target_pairs={{8,0},{16,8},{24,16},{32,24},{40,32},{48,40},{56,48},{64,56},{72,6... | collective-permute-start | bytes 98312 | tf_op jit(solution)/shard_map/ppermute | solution.py:26
  62.3 1.0 collective-permute-done.10
  63.3 5.1 %collective-permute-start.11 = (bf16[128,128]{1,0:T(8,128)(2,1)S(1)}, bf16[128,128]{1,0:T(8,128)(2,1)S(1)}, u32[]{:S(2)}, u32[]{:S(2)}) collective-permute-start(bf16[128,128]{1,0:T(8,128)(2,1)S(1)} %collective-permute-done.10), channel_id=1, source_target_pairs={{8,0},{16,8},{24,16},{32,24},{40,32},{48,40},{56,48},{64,56},{72,6... | collective-permute-start | bytes 98312 | tf_op jit(solution)/shard_map/ppermute | solution.py:26
  69.4 5.1 %collective-permute-start.12 = (bf16[128,128]{1,0:T(8,128)(2,1)S(1)}, bf16[128,128]{1,0:T(8,128)(2,1)S(1)}, u32[]{:S(2)}, u32[]{:S(2)}) collective-permute-start(bf16[128,128]{1,0:T(8,128)(2,1)S(1)} %collective-permute-done.11), channel_id=1, source_target_pairs={{8,0},{16,8},{24,16},{32,24},{40,32},{48,40},{56,48},{64,56},{72,6... | collective-permute-start | bytes 98312 | tf_op jit(solution)/shard_map/ppermute | solution.py:26
  74.4 1.0 collective-permute-done.12
  75.4 5.1 %collective-permute-start.13 = (bf16[128,128]{1,0:T(8,128)(2,1)S(1)}, bf16[128,128]{1,0:T(8,128)(2,1)S(1)}, u32[]{:S(2)}, u32[]{:S(2)}) collective-permute-start(bf16[128,128]{1,0:T(8,128)(2,1)S(1)} %collective-permute-done.12), channel_id=1, source_target_pairs={{8,0},{16,8},{24,16},{32,24},{40,32},{48,40},{56,48},{64,56},{72,6... | collective-permute-start | bytes 98312 | tf_op jit(solution)/shard_map/ppermute | solution.py:26
  80.7 0.8 collective-permute-done.13
  81.5 5.1 %collective-permute-start.14 = (bf16[128,128]{1,0:T(8,128)(2,1)S(1)}, bf16[128,128]{1,0:T(8,128)(2,1)S(1)}, u32[]{:S(2)}, u32[]{:S(2)}) collective-permute-start(bf16[128,128]{1,0:T(8,128)(2,1)S(1)} %collective-permute-done.13), channel_id=1, source_target_pairs={{8,0},{16,8},{24,16},{32,24},{40,32},{48,40},{56,48},{64,56},{72,6... | collective-permute-start | bytes 98312 | tf_op jit(solution)/shard_map/ppermute | solution.py:26
  87.2 0.6 constant_dynamic-update-slice_fusion.14
  87.8 0.6 constant_dynamic-update-slice_fusion.13
  88.4 0.6 constant_dynamic-update-slice_fusion.12
  89.1 0.6 constant_dynamic-update-slice_fusion.11
  89.7 0.6 constant_dynamic-update-slice_fusion.10
  90.3 0.6 constant_dynamic-update-slice_fusion.9
  90.9 0.6 constant_dynamic-update-slice_fusion.8
  91.5 0.6 constant_dynamic-update-slice_fusion.7
  92.1 0.6 constant_dynamic-update-slice_fusion.6
  94.0 0.6 constant_dynamic-update-slice_fusion.3
  94.6 0.6 constant_dynamic-update-slice_fusion.2
  95.2 0.6 constant_dynamic-update-slice_fusion.1
  95.8 0.6 constant_dynamic-update-slice_fusion
  96.4 1.7 gather_fusion
  98.1 2.8 fusion.3
  101.4 126.5 %all-reduce.3.cloned.1.call-done = f32[128,2048]{1,0:T(8,128)} async-done(((f32[128,2048]{1,0:T(8,128)}), f32[128,2048]{1,0:T(8,128)}) %all-reduce.3.cloned.1.call-update) | async-done | bytes 1048592 | tf_op jit(solution)/shard_map/psum | solution.py:109
  227.9 1.0 fusion.35
  230.0 1.2 broadcast_in_dim.20
  231.2 63.0 %all_to_all.10 = bf16[128,4,2048]{2,1,0:T(4,128)(2,1)S(1)} all-to-all(bf16[128,4,2048]{2,1,0:T(4,128)(2,1)S(1)} %bitcast.64), channel_id=1, replica_groups=mesh['section'=2,'seq'=16,'exp'=8] {'seq','exp'}, dimensions={0} | all-to-all | bytes 4194304 | tf_op jit(solution)/shard_map/all_to_all | solution.py:139
  294.3 2.1 reshape.138
  296.3 3.5 fusion.10
  299.9 5.0 %convolution_convert_fusion = bf16[512,2048]{1,0:T(8,128)(2,1)} fusion(bf16[512,2048]{1,0:T(8,128)(2,1)S(1)} %copy-done.1, bf16[1,256,2048]{2,1,0:T(8,128)(2,1)S(1)} %copy-done, bf16[1,2048,256]{2,1,0:T(8,128)(2,1)} %param.24, f32[512,256]{1,0:T(8,128)} %fusion.10), kind=kOutput, calls=%fused_computation.2 | convolution fusion | flops 1075576832 | bytes 6815744 | tf_op jit(solution)/shard_map/dot_general | solution.py:145
  304.9 4.1 %reshape.139 = bf16[128,4,2048]{2,1,0:T(4,128)(2,1)} reshape(bf16[512,2048]{1,0:T(8,128)(2,1)} %convolution_convert_fusion) | data formatting | bytes 4194304 | tf_op jit(solution)/shard_map/reshape | solution.py:147
  309.0 6.7 %all-to-all-start.1 = ((bf16[128,4,2048]{2,1,0:T(4,128)(2,1)}), bf16[128,4,2048]{2,1,0:T(4,128)(2,1)S(1)}, u32[]{:S(2)}, u32[]{:S(2)}) async-start(bf16[128,4,2048]{2,1,0:T(4,128)(2,1)} %reshape.139), calls=%async_computation.1 | async-start | bytes 4194304 | tf_op jit(solution)/shard_map/all_to_all | solution.py:144
  316.4 49.3 %all-to-all-done.1 = bf16[128,4,2048]{2,1,0:T(4,128)(2,1)S(1)} async-done(((bf16[128,4,2048]{2,1,0:T(4,128)(2,1)}), bf16[128,4,2048]{2,1,0:T(4,128)(2,1)S(1)}, u32[]{:S(2)}, u32[]{:S(2)}) %all-to-all-start.1) | async-done | bytes 2097184 | tf_op jit(solution)/shard_map/all_to_all | solution.py:144
  365.7 2.7 convert_reduce_fusion
  368.4 2.0 reshape.140
  370.4 1.8 fusion.81
  372.2 26.6 %all-reduce.5.cloned.1.call-done = f32[16,2048]{1,0:T(8,128)} async-done(((f32[16,2048]{1,0:T(8,128)}), f32[16,2048]{1,0:T(8,128)}) %all-reduce.5.cloned.1.call-update) | async-done | bytes 131088 | tf_op jit(solution)/shard_map/psum | solution.py:157
  398.8 1.5 fusion.38
  (68 shorter events, 6.5 us)
Async XLA Ops:
  6.5 293.3 %copy-start = (bf16[1,256,2048]{2,1,0:T(8,128)(2,1)S(1)}, bf16[1,256,2048]{2,1,0:T(8,128)(2,1)}, u32[]{:S(2)}) copy-start(bf16[1,256,2048]{2,1,0:T(8,128)(2,1)} %param.25) | copy-start | bytes 3145732
  6.5 10.6 %copy-start.2 = (bf16[128,2048]{1,0:T(8,128)(2,1)S(1)}, bf16[128,2048]{1,0:T(8,128)(2,1)}, u32[]{:S(2)}) copy-start(bf16[128,2048]{1,0:T(8,128)(2,1)} %param.13) | copy-start | bytes 1572868
  6.5 10.6 %copy-start.8 = (f32[2048]{0:T(1024)S(1)}, f32[2048]{0:T(1024)}, u32[]{:S(2)}) copy-start(f32[2048]{0:T(1024)} %param.15) | copy-start | bytes 24580
  6.5 10.6 %copy-start.7 = (bf16[2048,128]{1,0:T(8,128)(2,1)S(1)}, bf16[2048,128]{1,0:T(8,128)(2,1)}, u32[]{:S(2)}) copy-start(bf16[2048,128]{1,0:T(8,128)(2,1)} %param.16) | copy-start | bytes 1572868
  6.5 221.3 %all-reduce.3.cloned.1.call-start = ((), (), s32[]{:S(2)}) async-start(), calls=%async_computation.2 | async-start | bytes 2097152 | tf_op jit(solution)/shard_map/psum | solution.py:109
  8.0 30.8 %copy-start.4 = (s32[128]{0:T(128)S(1)}, s32[128]{0:T(128)}, u32[]{:S(2)}) copy-start(s32[128]{0:T(128)} %param.14) | copy-start | bytes 1540
  9.6 8.2 %collective-permute-start = (bf16[128,128]{1,0:T(8,128)(2,1)S(1)}, bf16[128,128]{1,0:T(8,128)(2,1)S(1)}, u32[]{:S(2)}, u32[]{:S(2)}) collective-permute-start(bf16[128,128]{1,0:T(8,128)(2,1)S(1)} %convolution_convert_fusion.2), channel_id=1, source_target_pairs={{0,8},{8,16},{16,24},{24,32},{32,40},{40,48},{48,56},{56,64},{64,7... | collective-permute-start | bytes 98312 | tf_op jit(solution)/shard_map/ppermute | solution.py:24
  11.8 42.9 %collective-permute-start.8 = (bf16[128,128]{1,0:T(8,128)(2,1)S(1)}, bf16[128,128]{1,0:T(8,128)(2,1)S(1)}, u32[]{:S(2)}, u32[]{:S(2)}) collective-permute-start(bf16[128,128]{1,0:T(8,128)(2,1)S(1)} %convolution_convert_fusion.2), channel_id=1, source_target_pairs={{8,0},{16,8},{24,16},{32,24},{40,32},{48,40},{56,48},{64,56},{72,6... | collective-permute-start | bytes 98312 | tf_op jit(solution)/shard_map/ppermute | solution.py:26
  17.6 63.0 %copy-start.5 = (s32[16,8]{0,1:T(8,128)S(1)}, s32[16,8]{0,1:T(8,128)}, u32[]{:S(2)}) copy-start(s32[16,8]{0,1:T(8,128)} %param.21) | copy-start | bytes 1540
  17.8 19.7 %collective-permute-start.1 = (bf16[128,128]{1,0:T(8,128)(2,1)S(1)}, bf16[128,128]{1,0:T(8,128)(2,1)S(1)}, u32[]{:S(2)}, u32[]{:S(2)}) collective-permute-start(bf16[128,128]{1,0:T(8,128)(2,1)S(1)} %collective-permute-done), channel_id=1, source_target_pairs={{0,8},{8,16},{16,24},{24,32},{32,40},{40,48},{48,56},{56,64},{64,7... | collective-permute-start | bytes 98312 | tf_op jit(solution)/shard_map/ppermute | solution.py:24
  37.5 18.7 %collective-permute-start.2 = (bf16[128,128]{1,0:T(8,128)(2,1)S(1)}, bf16[128,128]{1,0:T(8,128)(2,1)S(1)}, u32[]{:S(2)}, u32[]{:S(2)}) collective-permute-start(bf16[128,128]{1,0:T(8,128)(2,1)S(1)} %collective-permute-done.1), channel_id=1, source_target_pairs={{0,8},{8,16},{16,24},{24,32},{32,40},{40,48},{48,56},{56,64},{64,7... | collective-permute-start | bytes 98312 | tf_op jit(solution)/shard_map/ppermute | solution.py:24
  54.7 3.1 collective-permute-start.9
  56.2 6.1 %collective-permute-start.3 = (bf16[128,128]{1,0:T(8,128)(2,1)S(1)}, bf16[128,128]{1,0:T(8,128)(2,1)S(1)}, u32[]{:S(2)}, u32[]{:S(2)}) collective-permute-start(bf16[128,128]{1,0:T(8,128)(2,1)S(1)} %collective-permute-done.2), channel_id=1, source_target_pairs={{0,8},{8,16},{16,24},{24,32},{32,40},{40,48},{48,56},{56,64},{64,7... | collective-permute-start | bytes 98312 | tf_op jit(solution)/shard_map/ppermute | solution.py:24
  57.8 5.5 %collective-permute-start.10 = (bf16[128,128]{1,0:T(8,128)(2,1)S(1)}, bf16[128,128]{1,0:T(8,128)(2,1)S(1)}, u32[]{:S(2)}, u32[]{:S(2)}) collective-permute-start(bf16[128,128]{1,0:T(8,128)(2,1)S(1)} %collective-permute-done.9), channel_id=1, source_target_pairs={{8,0},{16,8},{24,16},{32,24},{40,32},{48,40},{56,48},{64,56},{72,6... | collective-permute-start | bytes 98312 | tf_op jit(solution)/shard_map/ppermute | solution.py:26
  62.3 6.1 %collective-permute-start.4 = (bf16[128,128]{1,0:T(8,128)(2,1)S(1)}, bf16[128,128]{1,0:T(8,128)(2,1)S(1)}, u32[]{:S(2)}, u32[]{:S(2)}) collective-permute-start(bf16[128,128]{1,0:T(8,128)(2,1)S(1)} %collective-permute-done.3), channel_id=1, source_target_pairs={{0,8},{8,16},{16,24},{24,32},{32,40},{40,48},{48,56},{56,64},{64,7... | collective-permute-start | bytes 98312 | tf_op jit(solution)/shard_map/ppermute | solution.py:24
  63.3 6.1 %collective-permute-start.11 = (bf16[128,128]{1,0:T(8,128)(2,1)S(1)}, bf16[128,128]{1,0:T(8,128)(2,1)S(1)}, u32[]{:S(2)}, u32[]{:S(2)}) collective-permute-start(bf16[128,128]{1,0:T(8,128)(2,1)S(1)} %collective-permute-done.10), channel_id=1, source_target_pairs={{8,0},{16,8},{24,16},{32,24},{40,32},{48,40},{56,48},{64,56},{72,6... | collective-permute-start | bytes 98312 | tf_op jit(solution)/shard_map/ppermute | solution.py:26
  68.3 6.1 %collective-permute-start.5 = (bf16[128,128]{1,0:T(8,128)(2,1)S(1)}, bf16[128,128]{1,0:T(8,128)(2,1)S(1)}, u32[]{:S(2)}, u32[]{:S(2)}) collective-permute-start(bf16[128,128]{1,0:T(8,128)(2,1)S(1)} %collective-permute-done.4), channel_id=1, source_target_pairs={{0,8},{8,16},{16,24},{24,32},{32,40},{40,48},{48,56},{56,64},{64,7... | collective-permute-start | bytes 98312 | tf_op jit(solution)/shard_map/ppermute | solution.py:24
  69.4 6.1 %collective-permute-start.12 = (bf16[128,128]{1,0:T(8,128)(2,1)S(1)}, bf16[128,128]{1,0:T(8,128)(2,1)S(1)}, u32[]{:S(2)}, u32[]{:S(2)}) collective-permute-start(bf16[128,128]{1,0:T(8,128)(2,1)S(1)} %collective-permute-done.11), channel_id=1, source_target_pairs={{8,0},{16,8},{24,16},{32,24},{40,32},{48,40},{56,48},{64,56},{72,6... | collective-permute-start | bytes 98312 | tf_op jit(solution)/shard_map/ppermute | solution.py:26
  74.4 6.1 %collective-permute-start.6 = (bf16[128,128]{1,0:T(8,128)(2,1)S(1)}, bf16[128,128]{1,0:T(8,128)(2,1)S(1)}, u32[]{:S(2)}, u32[]{:S(2)}) collective-permute-start(bf16[128,128]{1,0:T(8,128)(2,1)S(1)} %collective-permute-done.5), channel_id=1, source_target_pairs={{0,8},{8,16},{16,24},{24,32},{32,40},{40,48},{48,56},{56,64},{64,7... | collective-permute-start | bytes 98312 | tf_op jit(solution)/shard_map/ppermute | solution.py:24
  75.4 6.1 %collective-permute-start.13 = (bf16[128,128]{1,0:T(8,128)(2,1)S(1)}, bf16[128,128]{1,0:T(8,128)(2,1)S(1)}, u32[]{:S(2)}, u32[]{:S(2)}) collective-permute-start(bf16[128,128]{1,0:T(8,128)(2,1)S(1)} %collective-permute-done.12), channel_id=1, source_target_pairs={{8,0},{16,8},{24,16},{32,24},{40,32},{48,40},{56,48},{64,56},{72,6... | collective-permute-start | bytes 98312 | tf_op jit(solution)/shard_map/ppermute | solution.py:26
  80.5 6.1 %collective-permute-start.7 = (bf16[128,128]{1,0:T(8,128)(2,1)S(1)}, bf16[128,128]{1,0:T(8,128)(2,1)S(1)}, u32[]{:S(2)}, u32[]{:S(2)}) collective-permute-start(bf16[128,128]{1,0:T(8,128)(2,1)S(1)} %collective-permute-done.6), channel_id=1, source_target_pairs={{0,8},{8,16},{16,24},{24,32},{32,40},{40,48},{48,56},{56,64},{64,7... | collective-permute-start | bytes 98312 | tf_op jit(solution)/shard_map/ppermute | solution.py:24
  81.5 14.3 %collective-permute-start.14 = (bf16[128,128]{1,0:T(8,128)(2,1)S(1)}, bf16[128,128]{1,0:T(8,128)(2,1)S(1)}, u32[]{:S(2)}, u32[]{:S(2)}) collective-permute-start(bf16[128,128]{1,0:T(8,128)(2,1)S(1)} %collective-permute-done.13), channel_id=1, source_target_pairs={{8,0},{16,8},{24,16},{32,24},{40,32},{48,40},{56,48},{64,56},{72,6... | collective-permute-start | bytes 98312 | tf_op jit(solution)/shard_map/ppermute | solution.py:26
  98.1 130.8 %copy-start.3 = (f32[2048]{0:T(1024)S(1)}, f32[2048]{0:T(1024)}, u32[]{:S(2)}) copy-start(f32[2048]{0:T(1024)} %param.20) | copy-start | bytes 24580
  296.3 3.5 copy-start.1
  309.0 7.0 %copy-start.6 = (f32[16,8]{0,1:T(8,128)S(1)}, f32[16,8]{0,1:T(8,128)}, u32[]{:S(2)}) copy-start(f32[16,8]{0,1:T(8,128)} %param.22) | copy-start | bytes 1540
  309.0 56.7 %all-to-all-start.1 = ((bf16[128,4,2048]{2,1,0:T(4,128)(2,1)}), bf16[128,4,2048]{2,1,0:T(4,128)(2,1)S(1)}, u32[]{:S(2)}, u32[]{:S(2)}) async-start(bf16[128,4,2048]{2,1,0:T(4,128)(2,1)} %reshape.139), calls=%async_computation.1 | async-start | bytes 4194304 | tf_op jit(solution)/shard_map/all_to_all | solution.py:144
  315.7 83.0 %all-reduce.5.cloned.1.call-start = ((), (), s32[]{:S(2)}) async-start(), calls=%async_computation.3 | async-start | bytes 262144 | tf_op jit(solution)/shard_map/psum | solution.py:157
Sparse Core Ops, SparseCore 0:
  101.0 126.7 all-reduce.2
  372.3 26.4 all-reduce.4
